TPU v7x, 256 devices: a whole 4x4x8 slice. The times are simulated.
256 devices in a mesh: req: 32 (over z, x), head: 4 (over y), blk: 2 (over core).
Axes of the slice: x: 4, y: 4, z: 8, core: 2. Of those that a mesh axis runs over, the one named last changes fastest.
Arguments:
- x_tokens: bfloat16 [32, 512, 1024], P('req', ('head', 'blk')), may hold values from -40 to 40
- query: bfloat16 [32, 512, 1024], P('req', None, ('head', 'blk')), may hold values from -200 to 200
- key_new: bfloat16 [32, 512, 1024], P('req', None, ('head', 'blk')), may hold values from -4 to 4
- value_new: bfloat16 [32, 512, 1024], P('req', None, ('head', 'blk')), may hold values from -4 to 4
- cache_keys: bfloat16 [32, 2048, 1024], P('req', None, ('head', 'blk')), may hold values from -4 to 4
- cache_values: bfloat16 [32, 2048, 1024], P('req', None, ('head', 'blk')), may hold values from -4 to 4
- prefix_keys: bfloat16 [4, 512, 1024], P(None, None, ('head', 'blk')), may hold values from -4 to 4
- prefix_values: bfloat16 [4, 512, 1024], P(None, None, ('head', 'blk')), may hold values from -4 to 4
- history_len: int32 [32], P('req'), may hold values from 512 to 2048, as said below
- group_ids: int32 [32], P('req'), may hold values from 0 to 3
- out_weight: bfloat16 [1024, 1024], P(('head', 'blk')), may hold values from -0.1875 to 0.1875
- norm_gain: float32 [1024], replicated, may hold values from 0.5 to 1.5
- router_weight: bfloat16 [1024, 16], replicated, may hold values from -0.1875 to 0.1875
- expert_gate: bfloat16 [1024, 45056], P(None, ('req', 'head')), may hold values from -0.1875 to 0.1875
- expert_up: bfloat16 [1024, 45056], P(None, ('req', 'head')), may hold values from -0.1875 to 0.1875
- expert_down: bfloat16 [45056, 1024], P(('req', 'head')), may hold values from -0.109375 to 0.109375
- expert_ids: int32 [32, 512, 2], P('req', ('head', 'blk')), may hold values from 0 to 15, all different within a row; in each aligned block of 64 rows (0 to 63, 64 to 127, ..., all dimensions but the last counted through in order) at most 16 rows name the same one
- keep_mask: int32 [32, 512, 2], P('req', ('head', 'blk')), may hold values 0 or 1
Outputs:
- y_out: bfloat16 [32, 512, 1024], P('req', ('head', 'blk'))
- new_keys: bfloat16 [32, 2560, 1024], P('req', ('head', 'blk'))
- new_values: bfloat16 [32, 2560, 1024], P('req', ('head', 'blk'))
Inputs may be any that keep to these rules, and one draw needn't show every extreme that they name: `history_len`: one request has exactly 2048 used slots. `expert_ids`: the two experts of a token differ; within each aligned block of 64 tokens (one request, positions b * 64 onward) no expert is named by more than 16 choices, dropped ones included.
All inputs are finite; a program needn't handle non-finite values. No bound on the sum of `keep_mask` on one device may be relied on, other than what follows from the above.
Results may differ from a plain program's by a relative error of at most 0.0036.
Values may be sent and summed in bfloat16 or wider, within the bound.
No kernel may reach another device: no remote copies, remote signals or barrier semaphores. Data moves between devices by JAX's collectives and lax.ppermute only.
A program may use at most 64 MiB of HBM per device.

v0:
```python
import jax
import jax.numpy as jnp
from jax import lax
from jax.sharding import PartitionSpec as P

HD = 64
SLOT = 16
EPSILON = 1e-06


def attend_request(operands):
    (
        queries,
        keys_stretch,
        values_stretch,
        keys_cache,
        values_cache,
        keys_prefix,
        values_prefix,
        length,
    ) = operands
    heads_here = queries.shape[1] // HD
    prefix_rows = keys_prefix.shape[0]
    history_rows = keys_cache.shape[0]
    stretch_rows = queries.shape[0]
    keys_all = jnp.concatenate([keys_prefix, keys_cache, keys_stretch], 0).reshape(
        -1, heads_here, HD
    )
    values_all = jnp.concatenate([values_prefix, values_cache, values_stretch], 0).reshape(
        -1, heads_here, HD
    )
    key_pos = jnp.arange(keys_all.shape[0])
    query_pos = jnp.arange(stretch_rows)
    in_prefix = key_pos < prefix_rows
    in_history = (
        (key_pos >= prefix_rows)
        & (key_pos < prefix_rows + history_rows)
        & (key_pos - prefix_rows < length)
    )
    in_stretch = (key_pos[None, :] >= prefix_rows + history_rows) & (
        key_pos[None, :] - prefix_rows - history_rows <= query_pos[:, None]
    )
    visible = (in_prefix | in_history)[None, :] | in_stretch
    scores = jnp.einsum(
        "qhd,khd->hqk",
        queries.reshape(stretch_rows, heads_here, HD),
        keys_all,
        preferred_element_type=jnp.float32,
    ) * HD ** (-0.5)
    highest = jnp.max(jnp.where(visible[None], scores, -jnp.inf), axis=-1, keepdims=True)
    weights = jnp.where(visible[None], jnp.exp(scores - highest), 0.0)
    total = jnp.sum(weights, axis=-1, keepdims=True)
    rounded = weights.astype(jnp.bfloat16)
    mixed = jnp.einsum(
        "hqk,khd->qhd", rounded, values_all, preferred_element_type=jnp.float32
    ) / jnp.transpose(total, (1, 0, 2))
    return mixed.reshape(stretch_rows, -1).astype(jnp.bfloat16)


def extend(cache, stretch, length):
    hist = cache.shape[0]
    rows = stretch.shape[0]
    width = cache.shape[1]
    span = jnp.arange(hist + rows)
    padded_cache = jnp.concatenate([cache, jnp.zeros((rows, width), cache.dtype)], 0)
    framed = jnp.concatenate(
        [jnp.zeros((hist, width), stretch.dtype), stretch, jnp.zeros((hist, width), stretch.dtype)],
        0,
    )
    shifted = lax.dynamic_slice(framed, (hist - length, jnp.int32(0)), (hist + rows, width))
    return jnp.where((span < length)[:, None], padded_cache, shifted)


def to_positions(grown):
    groups = lax.axis_size(("head", "blk"))
    lead, rows, width = grown.shape
    parts = grown.reshape(lead, groups, rows // groups, width)
    got = lax.all_to_all(parts, ("head", "blk"), split_axis=1, concat_axis=1, tiled=True)
    return jnp.transpose(got, (0, 2, 1, 3)).reshape(lead, rows // groups, groups * width)


def body(
    x_tokens,
    query,
    key_new,
    value_new,
    cache_keys,
    cache_values,
    prefix_keys,
    prefix_values,
    history_len,
    group_ids,
    out_weight,
    norm_gain,
    router_weight,
    expert_gate,
    expert_up,
    expert_down,
    expert_ids,
    keep_mask,
):
    grown_keys = jax.vmap(extend)(cache_keys, key_new, history_len)
    grown_values = jax.vmap(extend)(cache_values, value_new, history_len)
    new_keys = to_positions(grown_keys)
    new_values = to_positions(grown_values)
    chosen_keys = jnp.take(prefix_keys, group_ids, axis=0)
    chosen_values = jnp.take(prefix_values, group_ids, axis=0)
    attended = lax.map(
        attend_request,
        (
            query,
            key_new,
            value_new,
            cache_keys,
            cache_values,
            chosen_keys,
            chosen_values,
            history_len,
        ),
    )
    requests_here = x_tokens.shape[0]
    rows_here = x_tokens.shape[1]
    width = x_tokens.shape[2]
    full_weight = lax.all_gather(out_weight, ("head", "blk"), axis=0, tiled=True)
    by_token = lax.all_to_all(attended, ("head", "blk"), split_axis=1, concat_axis=2, tiled=True)
    projected = jnp.einsum("rqf,fd->rqd", by_token, full_weight, preferred_element_type=jnp.float32)
    resid = x_tokens.astype(jnp.float32) + projected
    mean_square = jnp.mean(resid * resid, axis=-1, keepdims=True)
    normed = (resid * lax.rsqrt(mean_square + EPSILON) * norm_gain).astype(jnp.bfloat16)
    logits = jnp.dot(normed.reshape(-1, width), router_weight, preferred_element_type=jnp.float32)
    picks = expert_ids.reshape(-1, 2)
    chosen = jnp.take_along_axis(logits, picks, axis=1)
    keep = keep_mask.reshape(-1, 2)
    gate_weights = jax.nn.sigmoid(chosen - chosen[:, ::-1]) * keep.astype(jnp.float32)
    experts = router_weight.shape[1]
    slots_here = requests_here * SLOT
    block_picks = expert_ids.reshape(requests_here, rows_here * 2)
    onehot = (block_picks[:, :, None] == jnp.arange(experts)[None, None, :]).astype(jnp.int32)
    ranks = jnp.sum((jnp.cumsum(onehot, axis=1) - 1) * onehot, axis=-1)
    places = (block_picks * slots_here + jnp.arange(requests_here)[:, None] * SLOT + ranks).reshape(
        -1
    )
    sent_rows = (normed[:, :, None, :] * keep_mask[:, :, :, None].astype(jnp.bfloat16)).reshape(
        -1, width
    )
    buffer = jnp.zeros((experts * slots_here, width), jnp.bfloat16).at[places].set(sent_rows)
    holders = lax.axis_size("req") // experts
    outgoing = jnp.repeat(buffer.reshape(experts, slots_here, width), holders, axis=0)
    arrived = lax.all_to_all(outgoing, "req", split_axis=0, concat_axis=0, tiled=True)
    gathered = lax.all_gather(arrived, "head", axis=0, tiled=False)
    flat_rows = gathered.reshape(-1, width)
    gate_val = jnp.dot(flat_rows, expert_gate, preferred_element_type=jnp.float32)
    up_val = jnp.dot(flat_rows, expert_up, preferred_element_type=jnp.float32)
    hidden = (jax.nn.gelu(gate_val, approximate=True) * up_val).astype(jnp.bfloat16)
    partial = (
        jnp.dot(hidden, expert_down, preferred_element_type=jnp.float32)
        .astype(jnp.bfloat16)
        .reshape(gathered.shape)
    )
    shard_parts = lax.all_to_all(partial, "head", split_axis=0, concat_axis=0, tiled=True)
    half_sum = jnp.sum(shard_parts.astype(jnp.float32), axis=0).astype(jnp.bfloat16)
    returned = lax.all_to_all(half_sum, "req", split_axis=0, concat_axis=0, tiled=True)
    combined = jnp.sum(
        returned.reshape(experts, holders, slots_here, width), axis=1, dtype=jnp.float32
    ).reshape(experts * slots_here, width)
    picked = jnp.take(combined, places, axis=0).reshape(-1, 2, width)
    mixture = jnp.sum(picked * gate_weights[:, :, None], axis=1)
    y_out = (
        (resid.reshape(-1, width) + mixture)
        .astype(jnp.bfloat16)
        .reshape(requests_here, rows_here, width)
    )
    return (y_out, new_keys, new_values)


def solution(mesh):
    return jax.shard_map(
        body,
        mesh=mesh,
        in_specs=(
            P("req", ("head", "blk"), None),
            P("req", None, ("head", "blk")),
            P("req", None, ("head", "blk")),
            P("req", None, ("head", "blk")),
            P("req", None, ("head", "blk")),
            P("req", None, ("head", "blk")),
            P(None, None, ("head", "blk")),
            P(None, None, ("head", "blk")),
            P("req"),
            P("req"),
            P(("head", "blk"), None),
            P(),
            P(),
            P(None, ("req", "head")),
            P(None, ("req", "head")),
            P(("req", "head"), None),
            P("req", ("head", "blk"), None),
            P("req", ("head", "blk"), None),
        ),
        out_specs=(
            P("req", ("head", "blk"), None),
            P("req", ("head", "blk"), None),
            P("req", ("head", "blk"), None),
        ),
        check_vma=False,
    )
```

profile of v0, /device:TPU:2, one launch (start us, length us, event | category | flops | bytes accessed | tf_op | source)
XLA Modules:
  0.0 273.6 jit_solution(18118193608281846395)
XLA Ops:
  8.6 1.0 dynamic-slice_select_fusion
  10.4 1.2 copy.101
  11.6 1.0 copy.102
  12.6 1.0 copy.103
  14.2 4.3 %fusion.10 = pred[512,3072]{0,1:T(8,128)(4,1)} fusion(s32[3072]{0:T(1024)S(1)} %iota_add_fusion, pred[3072]{0:T(1024)(128)(4,1)S(1)} %get-tuple-element.73, pred[3072]{0:T(1024)(128)(4,1)S(1)} %get-tuple-element.74), kind=kLoop, calls=%fused_computation.16 | loop fusion | flops 4718592 | bytes 1591296 | tf_op jit(solution)/shard_map/while/body/eval_jaxpr/or | solution.py:43
  18.5 9.0 %fusion.72 = (f32[2,512]{1,0:T(2,128)S(1)}, bf16[2,512,3072]{1,2,0:T(8,128)(2,1)}) fusion(pred[512,3072]{0,1:T(8,128)(4,1)} %fusion.10, bf16[512,2,64]{0,2,1:T(8,128)(2,1)S(1)} %bitcast.130, bf16[512,2,64]{0,2,1:T(8,128)(2,1)S(1)} %bitcast.129, bf16[2048,2,64]{0,2,1:T(8,128)(2,1)S(1)} %bitcast.124, bf16[512,2,64]{0,2,1:T(8,128)(2,1)S(1)} %bitcast.126), kind=kOutput, calls=%fused_computation.108 | convolution fusion | flops 832048128 | bytes 8785920 | tf_op jit(solution)/shard_map/while/body/eval_jaxpr/sub | solution.py:51
  27.5 4.0 %fusion.29 = bf16[512,2,64]{0,2,1:T(8,128)(2,1)S(1)} fusion(bf16[2,512,3072]{1,2,0:T(8,128)(2,1)} %get-tuple-element.70, bf16[512,2,64]{0,2,1:T(8,128)(2,1)S(1)} %bitcast.128, bf16[2048,2,64]{0,2,1:T(8,128)(2,1)S(1)} %bitcast.123, bf16[512,2,64]{0,2,1:T(8,128)(2,1)S(1)} %bitcast.127, f32[512,2]{0,1:T(2,128)S(1)} %bitcast.133), kind=kOutput, calls=%fused_computation.39 | convolution fusion | flops 405143552 | bytes 7213056 | tf_op jit(solution)/shard_map/while/body/eval_jaxpr/hqk,khd->qhd/dot_general | solution.py:54
  32.2 1.4 reduce.3
  33.6 0.7 reshape.530
  34.3 4.6 %all-to-all-start = ((bf16[8,2,4096]{2,1,0:T(2,128)(2,1)}), bf16[8,2,4096]{2,1,0:T(2,128)(2,1)S(1)}, u32[]{:S(2)}, u32[]{:S(2)}) async-start(bf16[8,2,4096]{2,1,0:T(2,128)(2,1)} %reshape.530), calls=%async_computation | async-start | bytes 262144 | tf_op jit(solution)/shard_map/all_to_all | solution.py:125
  40.2 4.8 %all-to-all-done = bf16[8,2,4096]{2,1,0:T(2,128)(2,1)S(1)} async-done(((bf16[8,2,4096]{2,1,0:T(2,128)(2,1)}), bf16[8,2,4096]{2,1,0:T(2,128)(2,1)S(1)}, u32[]{:S(2)}, u32[]{:S(2)}) %all-to-all-start) | async-done | bytes 131104 | tf_op jit(solution)/shard_map/all_to_all | solution.py:125
  45.3 2.2 multiply_reduce_fusion.1
  47.5 0.7 copy-done.1
  49.2 1.4 scatter_custom_fusion
  50.7 39.4 %all_to_all.40 = bf16[32,16,1024]{2,1,0:T(8,128)(2,1)} all-to-all(bf16[32,16,1024]{2,1,0:T(8,128)(2,1)S(1)} %bitcast.117), channel_id=1, replica_groups=mesh['req'=32,'head'=4,'blk'=2] {'req'}, dimensions={0} | all-to-all | bytes 2097152 | tf_op jit(solution)/shard_map/all_to_all | solution.py:149
  90.3 6.3 %fusion.42 = (bf16[1,2560,128]{2,1,0:T(8,128)(2,1)}, bf16[1,2560,128]{2,1,0:T(8,128)(2,1)}) fusion(s32[]{:T(128)} %bitcast.33, bf16[1,2048,128]{2,1,0:T(8,128)(2,1)S(1)} %broadcast.289, bf16[1,512,128]{2,1,0:T(8,128)(2,1)S(1)} %copy-done.8, bf16[1,2048,128]{2,1,0:T(8,128)(2,1)S(1)} %copy-done.4, pred[2560]{0:T(1024)(128)(4,1)S(1)} %iota_compare_fusion.4, ...), kind=kLoop, calls=%fused_computation.51 | loop fusion | flops 4587520 | bytes 3148292 | tf_op jit(solution)/shard_map/vmap(jit(_where))/select_n | solution.py:71
  96.6 3.5 %all-to-all-start.5 = ((bf16[1,8,320,128]{3,2,0,1:T(8,128)(2,1)}), bf16[1,8,320,128]{3,2,0,1:T(8,128)(2,1)S(1)}, u32[]{:S(2)}, u32[]{:S(2)}) async-start(bf16[1,8,320,128]{3,2,0,1:T(8,128)(2,1)} %bitcast.36), calls=%async_computation.5 | async-start | bytes 1310720 | tf_op jit(solution)/shard_map/all_to_all | solution.py:78
  100.2 42.8 %all-gather.6.cloned.1.call-done = bf16[128,16,1024]{2,1,0:T(8,128)(2,1)} async-done(((bf16[32,16,1024]{2,1,0:T(8,128)(2,1)}), bf16[128,16,1024]{2,1,0:T(8,128)(2,1)}) %all-gather.6.cloned.1.call-update) | async-done | bytes 4194320 | tf_op jit(solution)/shard_map/all_gather | solution.py:150
  143.0 5.6 %fusion.73 = f32[2048,352]{0,1:T(8,128)} fusion(bf16[2048,1024]{1,0:T(8,128)(2,1)} %bitcast.131, bf16[1024,352]{0,1:T(8,128)(2,1)S(1)} %copy-done.14), kind=kOutput, calls=%fused_computation.109 | convolution fusion | flops 1476395008 | bytes 7798784 | tf_op jit(solution)/shard_map/dot_general | solution.py:152
  148.6 9.2 %convolution_convert_fusion = bf16[2048,1024]{1,0:T(8,128)(2,1)} fusion(bf16[352,1024]{1,0:T(8,128)(2,1)S(1)} %copy-done, bf16[2048,1024]{1,0:T(8,128)(2,1)} %bitcast.132, bf16[1024,352]{0,1:T(8,128)(2,1)S(1)} %copy-done.15, f32[2048,352]{0,1:T(8,128)} %fusion.73), kind=kOutput, calls=%fused_computation.19 | convolution fusion | flops 2962096128 | bytes 12713984 | tf_op jit(solution)/shard_map/dot_general | solution.py:156
  157.9 54.6 %all_to_all.41 = bf16[4,32,16,1024]{3,2,1,0:T(8,128)(2,1)} all-to-all(bf16[4,32,16,1024]{3,2,1,0:T(8,128)(2,1)} %bitcast.116), channel_id=1, replica_groups=mesh['req'=32,'head'=4,'blk'=2] {'head'}, dimensions={0} | all-to-all | bytes 8388608 | tf_op jit(solution)/shard_map/all_to_all | solution.py:160
  212.4 3.5 %all-to-all-start.4 = ((bf16[1,8,320,128]{3,2,0,1:T(8,128)(2,1)}), bf16[1,8,320,128]{3,2,0,1:T(8,128)(2,1)S(1)}, u32[]{:S(2)}, u32[]{:S(2)}) async-start(bf16[1,8,320,128]{3,2,0,1:T(8,128)(2,1)} %bitcast.34), calls=%async_computation.4 | async-start | bytes 1310720 | tf_op jit(solution)/shard_map/all_to_all | solution.py:78
  216.0 4.4 %reduce_sum.69 = bf16[32,16,1024]{2,1,0:T(8,128)(2,1)} reduce(bf16[4,32,16,1024]{3,2,1,0:T(8,128)(2,1)} %all_to_all.41, bf16[]{:T(256)} %constant.108.clone.1), dimensions={0}, to_apply=%region_6.8 | reduce | flops 1572864 | bytes 5242882 | tf_op jit(solution)/shard_map/reduce_sum | solution.py:161
  220.4 7.2 %all-to-all-done.4 = bf16[1,8,320,128]{3,2,0,1:T(8,128)(2,1)S(1)} async-done(((bf16[1,8,320,128]{3,2,0,1:T(8,128)(2,1)}), bf16[1,8,320,128]{3,2,0,1:T(8,128)(2,1)S(1)}, u32[]{:S(2)}, u32[]{:S(2)}) %all-to-all-start.4) | async-done | bytes 655392 | tf_op jit(solution)/shard_map/all_to_all | solution.py:78
  227.6 8.5 %all-to-all-start.3 = ((bf16[32,16,1024]{2,1,0:T(8,128)(2,1)}), bf16[32,16,1024]{2,1,0:T(8,128)(2,1)S(1)}, u32[]{:S(2)}, u32[]{:S(2)}) async-start(bf16[32,16,1024]{2,1,0:T(8,128)(2,1)} %reduce_sum.69), calls=%async_computation.3 | async-start | bytes 2097152 | tf_op jit(solution)/shard_map/all_to_all | solution.py:162
  236.7 0.9 copy_bitcast_fusion
  237.7 0.9 copy_bitcast_fusion.1
  238.8 1.3 gather_fusion.1
  240.4 23.4 %all-to-all-done.3 = bf16[32,16,1024]{2,1,0:T(8,128)(2,1)S(1)} async-done(((bf16[32,16,1024]{2,1,0:T(8,128)(2,1)}), bf16[32,16,1024]{2,1,0:T(8,128)(2,1)S(1)}, u32[]{:S(2)}, u32[]{:S(2)}) %all-to-all-start.3) | async-done | bytes 1048608 | tf_op jit(solution)/shard_map/all_to_all | solution.py:162
  264.1 0.8 gather_fusion
  265.2 0.8 multiply_reduce_fusion
  266.1 0.7 fusion.44
  (84 shorter events, 6.3 us)
Async XLA Ops:
  7.2 141.5 %copy-start = (bf16[352,1024]{1,0:T(8,128)(2,1)S(1)}, bf16[352,1024]{1,0:T(8,128)(2,1)}, u32[]{:S(2)}) copy-start(bf16[352,1024]{1,0:T(8,128)(2,1)} %param.35) | copy-start | bytes 2162692
  7.2 6.6 %copy-start.4 = (bf16[1,2048,128]{2,1,0:T(8,128)(2,1)S(1)}, bf16[1,2048,128]{2,1,0:T(8,128)(2,1)}, u32[]{:S(2)}) copy-start(bf16[1,2048,128]{2,1,0:T(8,128)(2,1)} %param.25) | copy-start | bytes 1572868
  7.2 6.8 %copy-start.8 = (bf16[1,512,128]{2,1,0:T(8,128)(2,1)S(1)}, bf16[1,512,128]{2,1,0:T(8,128)(2,1)}, u32[]{:S(2)}) copy-start(bf16[1,512,128]{2,1,0:T(8,128)(2,1)} %param.23) | copy-start | bytes 393220
  7.2 38.1 %all-gather.4.cloned.1.call-start = ((), (), s32[]{:S(2)}) async-start(), calls=%async_computation.6 | async-start | bytes 2359296 | tf_op jit(solution)/shard_map/all_gather | solution.py:124
  27.5 11.5 %copy-start.11 = (s32[1,64,2]{1,2,0:T(2,128)S(1)}, s32[1,64,2]{1,2,0:T(2,128)}, u32[]{:S(2)}) copy-start(s32[1,64,2]{1,2,0:T(2,128)} %param.36) | copy-start | bytes 1540
  27.5 11.9 %copy-start.13 = (s32[1,64,2]{1,2,0:T(2,128)S(1)}, s32[1,64,2]{1,2,0:T(2,128)}, u32[]{:S(2)}) copy-start(s32[1,64,2]{1,2,0:T(2,128)} %param.37) | copy-start | bytes 1540
  31.5 13.8 %copy-start.9 = (bf16[1,64,1024]{2,1,0:T(8,128)(2,1)S(1)}, bf16[1,64,1024]{2,1,0:T(8,128)(2,1)}, u32[]{:S(2)}) copy-start(bf16[1,64,1024]{2,1,0:T(8,128)(2,1)} %param.20) | copy-start | bytes 393220
  31.5 16.7 %copy-start.12 = (f32[1024]{0:T(1024)S(1)}, f32[1024]{0:T(1024)}, u32[]{:S(2)}) copy-start(f32[1024]{0:T(1024)} %param.31) | copy-start | bytes 12292
  34.3 10.7 %all-to-all-start = ((bf16[8,2,4096]{2,1,0:T(2,128)(2,1)}), bf16[8,2,4096]{2,1,0:T(2,128)(2,1)S(1)}, u32[]{:S(2)}, u32[]{:S(2)}) async-start(bf16[8,2,4096]{2,1,0:T(2,128)(2,1)} %reshape.530), calls=%async_computation | async-start | bytes 262144 | tf_op jit(solution)/shard_map/all_to_all | solution.py:125
  38.9 104.1 %all-gather.6.cloned.1.call-start = ((), (), s32[]{:S(2)}) async-start(), calls=%async_computation.7 | async-start | bytes 5242880 | tf_op jit(solution)/shard_map/all_gather | solution.py:150
  47.5 0.7 copy-start.1
  48.3 0.7 copy-start.5
  49.2 41.1 %copy-start.3 = (bf16[1,2048,128]{2,1,0:T(8,128)(2,1)S(1)}, bf16[1,2048,128]{2,1,0:T(8,128)(2,1)}, u32[]{:S(2)}) copy-start(bf16[1,2048,128]{2,1,0:T(8,128)(2,1)} %param.24) | copy-start | bytes 1572868
  49.2 41.1 %copy-start.7 = (bf16[1,512,128]{2,1,0:T(8,128)(2,1)S(1)}, bf16[1,512,128]{2,1,0:T(8,128)(2,1)}, u32[]{:S(2)}) copy-start(bf16[1,512,128]{2,1,0:T(8,128)(2,1)} %param.22) | copy-start | bytes 393220
  90.2 52.9 %copy-start.14 = (bf16[1024,352]{0,1:T(8,128)(2,1)S(1)}, bf16[1024,352]{0,1:T(8,128)(2,1)}, u32[]{:S(2)}) copy-start(bf16[1024,352]{0,1:T(8,128)(2,1)} %param.33) | copy-start | bytes 2162692
  96.6 61.2 %all-to-all-start.5 = ((bf16[1,8,320,128]{3,2,0,1:T(8,128)(2,1)}), bf16[1,8,320,128]{3,2,0,1:T(8,128)(2,1)S(1)}, u32[]{:S(2)}, u32[]{:S(2)}) async-start(bf16[1,8,320,128]{3,2,0,1:T(8,128)(2,1)} %bitcast.36), calls=%async_computation.5 | async-start | bytes 1310720 | tf_op jit(solution)/shard_map/all_to_all | solution.py:78
  143.0 5.6 %copy-start.15 = (bf16[1024,352]{0,1:T(8,128)(2,1)S(1)}, bf16[1024,352]{0,1:T(8,128)(2,1)}, u32[]{:S(2)}) copy-start(bf16[1024,352]{0,1:T(8,128)(2,1)} %param.34) | copy-start | bytes 2162692
  212.4 15.2 %all-to-all-start.4 = ((bf16[1,8,320,128]{3,2,0,1:T(8,128)(2,1)}), bf16[1,8,320,128]{3,2,0,1:T(8,128)(2,1)S(1)}, u32[]{:S(2)}, u32[]{:S(2)}) async-start(bf16[1,8,320,128]{3,2,0,1:T(8,128)(2,1)} %bitcast.34), calls=%async_computation.4 | async-start | bytes 1310720 | tf_op jit(solution)/shard_map/all_to_all | solution.py:78
  220.4 18.2 %copy-start.6 = (bf16[64,1024]{1,0:T(8,128)(2,1)S(1)}, bf16[64,1024]{1,0:T(8,128)(2,1)}, u32[]{:S(2)}) copy-start(bf16[64,1024]{1,0:T(8,128)(2,1)} %copy-done.5) | copy-start | bytes 393220
  220.4 18.2 %copy-start.10 = (bf16[1024,16]{0,1:T(8,128)(2,1)S(1)}, bf16[1024,16]{0,1:T(8,128)(2,1)}, u32[]{:S(2)}) copy-start(bf16[1024,16]{0,1:T(8,128)(2,1)} %param.32) | copy-start | bytes 98308
  227.6 36.2 %all-to-all-start.3 = ((bf16[32,16,1024]{2,1,0:T(8,128)(2,1)}), bf16[32,16,1024]{2,1,0:T(8,128)(2,1)S(1)}, u32[]{:S(2)}, u32[]{:S(2)}) async-start(bf16[32,16,1024]{2,1,0:T(8,128)(2,1)} %reduce_sum.69), calls=%async_computation.3 | async-start | bytes 2097152 | tf_op jit(solution)/shard_map/all_to_all | solution.py:162
  264.1 2.0 copy-start.2
Sparse Core Ops, SparseCore 0:
  9.9 30.8 all-gather.3
  90.3 52.6 all-gather.5
where the time goes:
time: 274 us
  blocking collectives  94 us (34%)
  waiting for transfers between devices  79 us (29%)
  matrix products  30.2 us (11%)
  other arithmetic  21.2 us (8%)
  starting transfers between devices  20.2 us (7%)
  between operations  15.8 us (6%)
  local copies, waits for them, and re-layouts  13.2 us (5%)
    all_to_all x1, blocking collectives, body(): lax.all_to_all(partial, 'head', split_axis=0, concat_axis=0, tiled=True)  54.6 us
    all_gather x1, waiting for transfers between devices, body(): gathered = lax.all_gather(arrived, 'head', axis=0, tiled=False)  42.8 us
    all_to_all x1, blocking collectives, body(): lax.all_to_all(outgoing, 'req', split_axis=0, concat_axis=0, tiled=True)  39.4 us
    all_to_all x1, waiting for transfers between devices, body(): lax.all_to_all(half_sum, 'req', split_axis=0, concat_axis=0, tiled=True)  23.4 us
    dot_general x1, matrix products, body(): jnp.dot(hidden, expert_down, preferred_element_type=jnp.float32)  9.24 us
    sub x1, matrix products, attend_request(): weights = jnp.where(visible[None], jnp.exp(scores - highest), 0.0)  9.01 us
    all_to_all x1, starting transfers between devices, body(): lax.all_to_all(half_sum, 'req', split_axis=0, concat_axis=0, tiled=True)  8.47 us
    all_to_all x2, waiting for transfers between devices, to_positions(): lax.all_to_all(parts, ('head', 'blk'), split_axis=1, concat_axis=1, tiled...  7.23 us
  transfers between devices with their start and end apart: 6, of which 4 were waited for; matrix products, arithmetic and copies ran while one was open for 21% of the time, Pallas kernels for 0%

commit v1 on v0

--- a/solution.py
+++ b/solution.py
@@ -75,7 +75,15 @@
     groups = lax.axis_size(("head", "blk"))
     lead, rows, width = grown.shape
     parts = grown.reshape(lead, groups, rows // groups, width)
-    got = lax.all_to_all(parts, ("head", "blk"), split_axis=1, concat_axis=1, tiled=True)
+    got = jnp.concatenate(
+        lax.all_to_all(
+            jnp.stack(jnp.split(parts, lax.axis_size(("head", "blk")), axis=1)),
+            ("head", "blk"),
+            0,
+            0,
+        ),
+        axis=1,
+    )
     return jnp.transpose(got, (0, 2, 1, 3)).reshape(lead, rows // groups, groups * width)
 
 

time: 274 us -> 279 us (1.018)
  blocking collectives: 94 us -> 39.4 us
  waiting for transfers between devices: 79 us -> 118 us
  local copies, waits for them, and re-layouts: 13.2 us -> 27.4 us
  starting transfers between devices: 20.2 us -> 26.7 us
    all_to_all x1 -> x0, blocking collectives: 54.6 us -> none  [body(): lax.all_to_all(partial, 'head', split_axis=0, concat_axis=0, tiled=True)]
    all_to_all x2 -> x3, waiting for transfers between devices: 7.23 us -> 51.1 us  [the longest x1 43.9 us: body(): lax.all_to_all(partial, 'head', split_axis=0, concat_axis=0, tiled=True)]
    unnamed x42 -> x54, local copies, waits for them, and re-layouts: 6.45 us -> 18.2 us
    all_to_all x2 -> x3, starting transfers between devices: 7.08 us -> 12.1 us  [the longest x2 7.26 us: to_positions(): lax.all_to_all(jnp.stack(jnp.split(parts, lax.axis_size(('head', 'blk')),...]
    all_gather x1, waiting for transfers between devices: 42.8 us -> 38 us  [body(): gathered = lax.all_gather(arrived, 'head', axis=0, tiled=False)]
  transfers between devices with their start and end apart: 6 -> 7, of which waited for: 4 -> 5; matrix products, arithmetic and copies ran while one was open for 21% -> 25% of each run, Pallas kernels for 0% -> 0%
where the time goes in v1:
time: 279 us; the launch traced here: 278 us
  waiting for transfers between devices  118 us (42%)
  blocking collectives  39.4 us (14%)
  matrix products  31.1 us (11%)
  local copies, waits for them, and re-layouts  27.4 us (10%)
  starting transfers between devices  26.7 us (10%)
  other arithmetic  19.1 us (7%)
  between operations  15.8 us (6%)
    all_to_all x1, waiting for transfers between devices, body(): lax.all_to_all(partial, 'head', split_axis=0, concat_axis=0, tiled=True)  43.9 us
    all_to_all x1, blocking collectives, body(): lax.all_to_all(outgoing, 'req', split_axis=0, concat_axis=0, tiled=True)  39.4 us
    all_gather x1, waiting for transfers between devices, body(): gathered = lax.all_gather(arrived, 'head', axis=0, tiled=False)  38 us
    all_to_all x1, waiting for transfers between devices, body(): lax.all_to_all(half_sum, 'req', split_axis=0, concat_axis=0, tiled=True)  23.5 us
    unnamed x54, local copies, waits for them, and re-layouts  18.2 us
    all_to_all x1, starting transfers between devices, body(): lax.all_to_all(half_sum, 'req', split_axis=0, concat_axis=0, tiled=True)  10.1 us
    sub x1, matrix products, attend_request(): weights = jnp.where(visible[None], jnp.exp(scores - highest), 0.0)  9.48 us
    dot_general x1, matrix products, body(): jnp.dot(hidden, expert_down, preferred_element_type=jnp.float32)  9.24 us
  transfers between devices with their start and end apart: 7, of which 5 were waited for; matrix products, arithmetic and copies ran while one was open for 25% of the time, Pallas kernels for 0%

profile of v1, /device:TPU:2, one launch (start us, length us, event | category | flops | bytes accessed | tf_op | source)
XLA Modules:
  0.0 277.8 jit_solution(2917030886155649860)
XLA Ops:
  8.6 1.0 dynamic-slice_select_fusion
  9.6 0.8 copy.112
  11.0 2.0 copy.113
  13.0 1.7 copy.114
  14.7 1.7 copy.115
  17.4 0.8 copy.111
  18.1 2.8 %fusion.10 = pred[512,3072]{0,1:T(8,128)(4,1)S(1)} fusion(s32[3072]{0:T(1024)S(1)} %iota_add_fusion, pred[3072]{0:T(1024)(128)(4,1)S(1)} %get-tuple-element.73, pred[3072]{0:T(1024)(128)(4,1)S(1)} %get-tuple-element.74), kind=kLoop, calls=%fused_computation.16 | loop fusion | flops 4718592 | bytes 1591296 | tf_op jit(solution)/shard_map/while/body/eval_jaxpr/or | solution.py:43
  20.9 9.5 %fusion.88 = (f32[2,512]{1,0:T(2,128)S(1)}, bf16[2,512,3072]{1,2,0:T(8,128)(2,1)}) fusion(pred[512,3072]{0,1:T(8,128)(4,1)S(1)} %fusion.10, bf16[512,2,64]{0,2,1:T(8,128)(2,1)} %bitcast.214, bf16[512,2,64]{0,2,1:T(8,128)(2,1)} %bitcast.213, bf16[2048,2,64]{0,2,1:T(8,128)(2,1)} %bitcast.208, bf16[512,2,64]{0,2,1:T(8,128)(2,1)} %bitcast.210), kind=kOutput, calls=%fused_computation.140 | convolution fusion | flops 832048128 | bytes 8785920 | tf_op jit(solution)/shard_map/while/body/eval_jaxpr/sub | solution.py:51
  30.4 4.3 %fusion.29 = bf16[512,2,64]{0,2,1:T(8,128)(2,1)S(1)} fusion(bf16[2,512,3072]{1,2,0:T(8,128)(2,1)} %get-tuple-element.70, bf16[512,2,64]{0,2,1:T(8,128)(2,1)} %bitcast.212, bf16[2048,2,64]{0,2,1:T(8,128)(2,1)S(1)} %bitcast.207, bf16[512,2,64]{0,2,1:T(8,128)(2,1)} %bitcast.211, f32[512,2]{0,1:T(2,128)S(1)} %bitcast.217), kind=kOutput, calls=%fused_computation.39 | convolution fusion | flops 405143552 | bytes 7213056 | tf_op jit(solution)/shard_map/while/body/eval_jaxpr/hqk,khd->qhd/dot_general | solution.py:54
  35.4 1.4 reduce.3
  37.5 4.4 %all-to-all-start = ((bf16[8,2,4096]{2,1,0:T(2,128)(2,1)}), bf16[8,2,4096]{2,1,0:T(2,128)(2,1)S(1)}, u32[]{:S(2)}, u32[]{:S(2)}) async-start(bf16[8,2,4096]{2,1,0:T(2,128)(2,1)} %reshape.538), calls=%async_computation | async-start | bytes 262144 | tf_op jit(solution)/shard_map/all_to_all | solution.py:133
  43.2 4.8 %all-to-all-done = bf16[8,2,4096]{2,1,0:T(2,128)(2,1)S(1)} async-done(((bf16[8,2,4096]{2,1,0:T(2,128)(2,1)}), bf16[8,2,4096]{2,1,0:T(2,128)(2,1)S(1)}, u32[]{:S(2)}, u32[]{:S(2)}) %all-to-all-start) | async-done | bytes 131104 | tf_op jit(solution)/shard_map/all_to_all | solution.py:133
  48.3 2.2 multiply_reduce_fusion.1
  52.3 1.4 scatter_custom_fusion
  53.8 39.4 %all_to_all.40 = bf16[32,16,1024]{2,1,0:T(8,128)(2,1)} all-to-all(bf16[32,16,1024]{2,1,0:T(8,128)(2,1)S(1)} %bitcast.185), channel_id=1, replica_groups=mesh['req'=32,'head'=4,'blk'=2] {'req'}, dimensions={0} | all-to-all | bytes 2097152 | tf_op jit(solution)/shard_map/all_to_all | solution.py:157
  93.4 5.8 %fusion.42 = (bf16[1,2560,128]{2,1,0:T(8,128)(2,1)S(1)}, bf16[1,2560,128]{2,1,0:T(8,128)(2,1)S(1)}) fusion(s32[]{:T(128)} %bitcast.33, bf16[1,2048,128]{2,1,0:T(8,128)(2,1)S(1)} %broadcast.289, bf16[1,512,128]{2,1,0:T(8,128)(2,1)S(1)} %copy-done.8, bf16[1,2048,128]{2,1,0:T(8,128)(2,1)S(1)} %copy-done.4, pred[2560]{0:T(1024)(128)(4,1)S(1)} %iota_compare_fusion.4, ...), kind=kLoop, calls=%fused_computation.51 | loop fusion | flops 4587520 | bytes 3148292 | tf_op jit(solution)/shard_map/vmap(jit(_where))/select_n | solution.py:71
  104.3 3.7 %all-to-all-start.5 = ((bf16[8,1,1,320,128]{4,3,2,1,0:T(8,128)(2,1)}), bf16[8,1,1,320,128]{4,3,2,1,0:T(8,128)(2,1)S(1)}, u32[]{:S(2)}, u32[]{:S(2)}) async-start(bf16[8,1,1,320,128]{4,3,2,1,0:T(8,128)(2,1)} %fusion.52), calls=%async_computation.5 | async-start | bytes 1310720 | tf_op jit(solution)/shard_map/all_to_all | solution.py:79
  108.0 38.0 %all-gather.6.cloned.1.call-done = bf16[128,16,1024]{2,1,0:T(8,128)(2,1)} async-done(((bf16[32,16,1024]{2,1,0:T(8,128)(2,1)}), bf16[128,16,1024]{2,1,0:T(8,128)(2,1)}) %all-gather.6.cloned.1.call-update) | async-done | bytes 4194320 | tf_op jit(solution)/shard_map/all_gather | solution.py:158
  146.1 5.8 %fusion.89 = f32[2048,352]{0,1:T(8,128)} fusion(bf16[2048,1024]{1,0:T(8,128)(2,1)} %bitcast.215, bf16[1024,352]{0,1:T(8,128)(2,1)} %param.33), kind=kOutput, calls=%fused_computation.141 | convolution fusion | flops 1476395008 | bytes 7798784 | tf_op jit(solution)/shard_map/dot_general | solution.py:160
  151.9 9.2 %convolution_convert_fusion = bf16[2048,1024]{1,0:T(8,128)(2,1)} fusion(bf16[352,1024]{1,0:T(8,128)(2,1)S(1)} %copy-done, bf16[2048,1024]{1,0:T(8,128)(2,1)} %bitcast.216, bf16[1024,352]{0,1:T(8,128)(2,1)S(1)} %copy-done.14, f32[2048,352]{0,1:T(8,128)} %fusion.89), kind=kOutput, calls=%fused_computation.19 | convolution fusion | flops 2962096128 | bytes 12713984 | tf_op jit(solution)/shard_map/dot_general | solution.py:164
  161.1 4.8 %all-to-all-start.2 = ((bf16[4,32,16,1024]{3,2,1,0:T(8,128)(2,1)}), bf16[4,32,16,1024]{3,2,1,0:T(8,128)(2,1)}, u32[]{:S(2)}, u32[]{:S(2)}) async-start(bf16[4,32,16,1024]{3,2,1,0:T(8,128)(2,1)} %bitcast.184), calls=%async_computation.2 | async-start | bytes 8388608 | tf_op jit(solution)/shard_map/all_to_all | solution.py:168
  171.1 43.9 %all-to-all-done.2 = bf16[4,32,16,1024]{3,2,1,0:T(8,128)(2,1)} async-done(((bf16[4,32,16,1024]{3,2,1,0:T(8,128)(2,1)}), bf16[4,32,16,1024]{3,2,1,0:T(8,128)(2,1)}, u32[]{:S(2)}, u32[]{:S(2)}) %all-to-all-start.2) | async-done | bytes 4194336 | tf_op jit(solution)/shard_map/all_to_all | solution.py:168
  214.9 3.5 %all-to-all-start.4 = ((bf16[8,1,1,320,128]{4,3,2,1,0:T(8,128)(2,1)}), bf16[8,1,1,320,128]{4,3,2,1,0:T(8,128)(2,1)S(1)}, u32[]{:S(2)}, u32[]{:S(2)}) async-start(bf16[8,1,1,320,128]{4,3,2,1,0:T(8,128)(2,1)} %fusion.60), calls=%async_computation.4 | async-start | bytes 1310720 | tf_op jit(solution)/shard_map/all_to_all | solution.py:79
  218.5 4.4 %reduce_sum.69 = bf16[32,16,1024]{2,1,0:T(8,128)(2,1)} reduce(bf16[4,32,16,1024]{3,2,1,0:T(8,128)(2,1)} %all-to-all-done.2, bf16[]{:T(256)} %constant.108.clone.1), dimensions={0}, to_apply=%region_6.8 | reduce | flops 1572864 | bytes 5242882 | tf_op jit(solution)/shard_map/reduce_sum | solution.py:169
  222.9 7.2 %all-to-all-done.4 = bf16[8,1,1,320,128]{4,3,2,1,0:T(8,128)(2,1)S(1)} async-done(((bf16[8,1,1,320,128]{4,3,2,1,0:T(8,128)(2,1)}), bf16[8,1,1,320,128]{4,3,2,1,0:T(8,128)(2,1)S(1)}, u32[]{:S(2)}, u32[]{:S(2)}) %all-to-all-start.4) | async-done | bytes 655392 | tf_op jit(solution)/shard_map/all_to_all | solution.py:79
  230.1 10.1 %all-to-all-start.3 = ((bf16[32,16,1024]{2,1,0:T(8,128)(2,1)}), bf16[32,16,1024]{2,1,0:T(8,128)(2,1)S(1)}, u32[]{:S(2)}, u32[]{:S(2)}) async-start(bf16[32,16,1024]{2,1,0:T(8,128)(2,1)} %reduce_sum.69), calls=%async_computation.3 | async-start | bytes 2097152 | tf_op jit(solution)/shard_map/all_to_all | solution.py:170
  240.9 0.9 copy_bitcast_fusion
  241.8 0.9 copy_bitcast_fusion.1
  242.9 1.3 gather_fusion.1
  244.6 23.5 %all-to-all-done.3 = bf16[32,16,1024]{2,1,0:T(8,128)(2,1)S(1)} async-done(((bf16[32,16,1024]{2,1,0:T(8,128)(2,1)}), bf16[32,16,1024]{2,1,0:T(8,128)(2,1)S(1)}, u32[]{:S(2)}, u32[]{:S(2)}) %all-to-all-start.3) | async-done | bytes 1048608 | tf_op jit(solution)/shard_map/all_to_all | solution.py:170
  268.3 0.8 gather_fusion
  269.4 0.8 multiply_reduce_fusion
  (99 shorter events, 19.0 us)
Async XLA Ops:
  7.2 144.7 %copy-start = (bf16[352,1024]{1,0:T(8,128)(2,1)S(1)}, bf16[352,1024]{1,0:T(8,128)(2,1)}, u32[]{:S(2)}) copy-start(bf16[352,1024]{1,0:T(8,128)(2,1)} %param.35) | copy-start | bytes 2162692
  7.2 9.9 %copy-start.4 = (bf16[1,2048,128]{2,1,0:T(8,128)(2,1)S(1)}, bf16[1,2048,128]{2,1,0:T(8,128)(2,1)}, u32[]{:S(2)}) copy-start(bf16[1,2048,128]{2,1,0:T(8,128)(2,1)} %param.25) | copy-start | bytes 1572868
  7.2 10.2 %copy-start.8 = (bf16[1,512,128]{2,1,0:T(8,128)(2,1)S(1)}, bf16[1,512,128]{2,1,0:T(8,128)(2,1)}, u32[]{:S(2)}) copy-start(bf16[1,512,128]{2,1,0:T(8,128)(2,1)} %param.23) | copy-start | bytes 393220
  7.2 41.1 %all-gather.4.cloned.1.call-start = ((), (), s32[]{:S(2)}) async-start(), calls=%async_computation.6 | async-start | bytes 2359296 | tf_op jit(solution)/shard_map/all_gather | solution.py:132
  30.4 11.6 %copy-start.11 = (s32[1,64,2]{1,2,0:T(2,128)S(1)}, s32[1,64,2]{1,2,0:T(2,128)}, u32[]{:S(2)}) copy-start(s32[1,64,2]{1,2,0:T(2,128)} %param.36) | copy-start | bytes 1540
  30.4 12.1 %copy-start.13 = (s32[1,64,2]{1,2,0:T(2,128)S(1)}, s32[1,64,2]{1,2,0:T(2,128)}, u32[]{:S(2)}) copy-start(s32[1,64,2]{1,2,0:T(2,128)} %param.37) | copy-start | bytes 1540
  34.7 13.6 %copy-start.9 = (bf16[1,64,1024]{2,1,0:T(8,128)(2,1)S(1)}, bf16[1,64,1024]{2,1,0:T(8,128)(2,1)}, u32[]{:S(2)}) copy-start(bf16[1,64,1024]{2,1,0:T(8,128)(2,1)} %param.20) | copy-start | bytes 393220
  34.7 16.5 %copy-start.12 = (f32[1024]{0:T(1024)S(1)}, f32[1024]{0:T(1024)}, u32[]{:S(2)}) copy-start(f32[1024]{0:T(1024)} %param.31) | copy-start | bytes 12292
  37.5 10.5 %all-to-all-start = ((bf16[8,2,4096]{2,1,0:T(2,128)(2,1)}), bf16[8,2,4096]{2,1,0:T(2,128)(2,1)S(1)}, u32[]{:S(2)}, u32[]{:S(2)}) async-start(bf16[8,2,4096]{2,1,0:T(2,128)(2,1)} %reshape.538), calls=%async_computation | async-start | bytes 262144 | tf_op jit(solution)/shard_map/all_to_all | solution.py:133
  42.0 104.1 %all-gather.6.cloned.1.call-start = ((), (), s32[]{:S(2)}) async-start(), calls=%async_computation.7 | async-start | bytes 5242880 | tf_op jit(solution)/shard_map/all_gather | solution.py:158
  50.5 0.7 copy-start.1
  51.3 0.7 copy-start.5
  52.3 41.1 %copy-start.3 = (bf16[1,2048,128]{2,1,0:T(8,128)(2,1)S(1)}, bf16[1,2048,128]{2,1,0:T(8,128)(2,1)}, u32[]{:S(2)}) copy-start(bf16[1,2048,128]{2,1,0:T(8,128)(2,1)} %param.24) | copy-start | bytes 1572868
  52.3 41.1 %copy-start.7 = (bf16[1,512,128]{2,1,0:T(8,128)(2,1)S(1)}, bf16[1,512,128]{2,1,0:T(8,128)(2,1)}, u32[]{:S(2)}) copy-start(bf16[1,512,128]{2,1,0:T(8,128)(2,1)} %param.22) | copy-start | bytes 393220
  104.3 56.8 %all-to-all-start.5 = ((bf16[8,1,1,320,128]{4,3,2,1,0:T(8,128)(2,1)}), bf16[8,1,1,320,128]{4,3,2,1,0:T(8,128)(2,1)S(1)}, u32[]{:S(2)}, u32[]{:S(2)}) async-start(bf16[8,1,1,320,128]{4,3,2,1,0:T(8,128)(2,1)} %fusion.52), calls=%async_computation.5 | async-start | bytes 1310720 | tf_op jit(solution)/shard_map/all_to_all | solution.py:79
  146.1 5.8 %copy-start.14 = (bf16[1024,352]{0,1:T(8,128)(2,1)S(1)}, bf16[1024,352]{0,1:T(8,128)(2,1)}, u32[]{:S(2)}) copy-start(bf16[1024,352]{0,1:T(8,128)(2,1)} %param.34) | copy-start | bytes 2162692
  161.1 53.8 %all-to-all-start.2 = ((bf16[4,32,16,1024]{3,2,1,0:T(8,128)(2,1)}), bf16[4,32,16,1024]{3,2,1,0:T(8,128)(2,1)}, u32[]{:S(2)}, u32[]{:S(2)}) async-start(bf16[4,32,16,1024]{3,2,1,0:T(8,128)(2,1)} %bitcast.184), calls=%async_computation.2 | async-start | bytes 8388608 | tf_op jit(solution)/shard_map/all_to_all | solution.py:168
  214.9 15.2 %all-to-all-start.4 = ((bf16[8,1,1,320,128]{4,3,2,1,0:T(8,128)(2,1)}), bf16[8,1,1,320,128]{4,3,2,1,0:T(8,128)(2,1)S(1)}, u32[]{:S(2)}, u32[]{:S(2)}) async-start(bf16[8,1,1,320,128]{4,3,2,1,0:T(8,128)(2,1)} %fusion.60), calls=%async_computation.4 | async-start | bytes 1310720 | tf_op jit(solution)/shard_map/all_to_all | solution.py:79
  222.9 19.9 %copy-start.6 = (bf16[64,1024]{1,0:T(8,128)(2,1)S(1)}, bf16[64,1024]{1,0:T(8,128)(2,1)}, u32[]{:S(2)}) copy-start(bf16[64,1024]{1,0:T(8,128)(2,1)} %copy-done.5) | copy-start | bytes 393220
  222.9 19.9 %copy-start.10 = (bf16[1024,16]{0,1:T(8,128)(2,1)S(1)}, bf16[1024,16]{0,1:T(8,128)(2,1)}, u32[]{:S(2)}) copy-start(bf16[1024,16]{0,1:T(8,128)(2,1)} %param.32) | copy-start | bytes 98308
  230.1 37.9 %all-to-all-start.3 = ((bf16[32,16,1024]{2,1,0:T(8,128)(2,1)}), bf16[32,16,1024]{2,1,0:T(8,128)(2,1)S(1)}, u32[]{:S(2)}, u32[]{:S(2)}) async-start(bf16[32,16,1024]{2,1,0:T(8,128)(2,1)} %reduce_sum.69), calls=%async_computation.3 | async-start | bytes 2097152 | tf_op jit(solution)/shard_map/all_to_all | solution.py:170
  268.3 2.0 copy-start.2
Sparse Core Ops, SparseCore 0:
  9.9 30.8 all-gather.3
  93.4 52.6 all-gather.5
